TPU v7x, 512 devices: a whole 4x8x8 slice. The times are simulated.
512 devices in a mesh: dp: 8 (over y), expert: 64 (over x, z, core).
Axes of the slice: x: 4, y: 8, z: 8, core: 2. Of those that a mesh axis runs over, the one named last changes fastest.
Arguments:
- tokens: bfloat16 [65536, 3584], P(('dp', 'expert')), may hold values from -6 to 6
- out_cotangent: bfloat16 [65536, 3584], P(('dp', 'expert')), may hold values from -6 to 6
- expert_ids: int32 [65536, 8], P(('dp', 'expert')), may hold values from 0 to 255, as said below
- gate_fixed: int32 [65536, 8], P(('dp', 'expert')), may hold values from 4096 to 65535
- w_gate: bfloat16 [64, 3584, 128], P('expert', 'dp'), may hold values from -0.09375 to 0.09375
- w_up: bfloat16 [64, 3584, 128], P('expert', 'dp'), may hold values from -0.09375 to 0.09375
- w_down: bfloat16 [64, 3584, 128], P('expert', 'dp'), may hold values from -0.125 to 0.125
Outputs:
- layer_out: bfloat16 [65536, 3584], P(('dp', 'expert'))
- token_grad: bfloat16 [65536, 3584], P(('dp', 'expert'))
- grad_gate: float32 [64, 3584, 128], P('expert', 'dp')
- grad_up: float32 [64, 3584, 128], P('expert', 'dp')
- grad_down: float32 [64, 3584, 128], P('expert', 'dp')
Inputs may be any that keep to these rules, and one draw needn't show every extreme that they name: `expert_ids`: each row names 8 different experts. Within the 128 rows of one device each expert below 4 is named by 1 to 4 rows; in every draw one expert below 4 is named by exactly 4 rows on every device.
All inputs are finite; a program needn't handle non-finite values.
Results may differ from a plain program's by a relative error of at most 0.014.
Values may be sent and summed in bfloat16 or wider, within the bound.
No kernel may reach another device: no remote copies, remote signals or barrier semaphores. Data moves between devices by JAX's collectives and lax.ppermute only.
A program may use at most 128 MiB of HBM per device.

v0:
```python
import jax
import jax.numpy as jnp
from jax import lax
from jax.sharding import PartitionSpec as P

SPLIT = 16
CAP = 4
SCALE = 2.0 ** (-16)
HIGH = lax.Precision.HIGHEST


def routing(ids, gates, window, capacity):
    wanted = jnp.arange(window, dtype=jnp.int32)
    hits = ids[:, :, None] == wanted[None, None, :]
    member = jnp.any(hits, axis=1)
    weight = jnp.sum(jnp.where(hits, gates[:, :, None], 0), axis=1).astype(jnp.float32) * SCALE
    rank = jnp.cumsum(member.astype(jnp.int32), axis=0) - 1
    slots = jnp.arange(capacity, dtype=jnp.int32)
    pick = jnp.logical_and(member[:, :, None], rank[:, :, None] == slots[None, None, :])
    select = jnp.where(pick, 1.0, 0.0).astype(jnp.float32)
    slot_gate = jnp.sum(select * weight[:, :, None], axis=0)
    return (select, slot_gate)


def expert_math(inputs, cotangents, gate_w, up_w, down_w):
    gate_pre = jnp.einsum("prf,pfh->rh", inputs, gate_w, preferred_element_type=jnp.float32)
    up_pre = jnp.einsum("prf,pfh->rh", inputs, up_w, preferred_element_type=jnp.float32)
    sig = jax.nn.sigmoid(gate_pre)
    act = gate_pre * sig
    hidden = (act * up_pre).astype(jnp.bfloat16)
    partial_out = jnp.einsum("rh,pfh->prf", hidden, down_w, preferred_element_type=jnp.float32)
    d_hidden = jnp.einsum("prf,pfh->rh", cotangents, down_w, preferred_element_type=jnp.float32)
    d_gate = (d_hidden * up_pre * sig * (1.0 + gate_pre * (1.0 - sig))).astype(jnp.bfloat16)
    d_up = (d_hidden * act).astype(jnp.bfloat16)
    partial_grad = jnp.einsum(
        "rh,pfh->prf", d_gate, gate_w, preferred_element_type=jnp.float32
    ) + jnp.einsum("rh,pfh->prf", d_up, up_w, preferred_element_type=jnp.float32)
    term = jnp.concatenate(
        [
            jnp.einsum("prf,rh->pfh", inputs, d_gate, preferred_element_type=jnp.float32),
            jnp.einsum("prf,rh->pfh", inputs, d_up, preferred_element_type=jnp.float32),
            jnp.einsum("prf,rh->pfh", cotangents, hidden, preferred_element_type=jnp.float32),
        ],
        axis=2,
    )
    return (partial_out, partial_grad, term.reshape(-1, term.shape[2]))


def per_device(tokens, out_cotangent, expert_ids, gate_fixed, w_gate, w_up, w_down):
    tok_rows, width = tokens.shape
    groups = lax.axis_size("expert")
    window = groups // SPLIT
    hid = w_gate.shape[2]
    parts = 1
    feat = width // parts
    select, slot_gate = routing(expert_ids, gate_fixed, window, CAP)
    select_b = select.astype(jnp.bfloat16)
    tok3 = tokens.reshape(tok_rows, parts, feat)
    cot3 = out_cotangent.reshape(tok_rows, parts, feat)
    slot_tokens = jnp.einsum(
        "tec,tsf->escf", select_b, tok3, preferred_element_type=jnp.float32
    ).astype(jnp.bfloat16)
    picked = jnp.einsum("tec,tsf->escf", select_b, cot3, preferred_element_type=jnp.float32)
    slot_cot = (picked * slot_gate[:, None, :, None]).astype(jnp.bfloat16)
    payload = jnp.stack([slot_tokens, slot_cot], axis=2)
    gate_full, up_full, down_full = (
        lax.all_gather(w_gate, "dp", axis=1, tiled=True),
        lax.all_gather(w_up, "dp", axis=1, tiled=True),
        lax.all_gather(w_down, "dp", axis=1, tiled=True),
    )
    outgoing = jnp.broadcast_to(payload, (window, SPLIT, 2, CAP, width)).reshape(
        groups, 2, CAP, width
    )
    arrived = lax.all_to_all(outgoing, "expert", split_axis=0, concat_axis=0, tiled=True)
    pieces = arrived[None]
    inputs = pieces[:, :, 0].reshape(parts, groups * CAP, feat)
    cotangents = pieces[:, :, 1].reshape(parts, groups * CAP, feat)
    partial_out, partial_grad, term = expert_math(inputs, cotangents, gate_full, up_full, down_full)
    summed = lax.psum_scatter(
        term.astype(jnp.bfloat16), "dp", scatter_dimension=0, tiled=True
    ).astype(jnp.float32)
    grad_gate = summed[:, :hid][None]
    grad_up = summed[:, hid : 2 * hid][None]
    grad_down = summed[:, 2 * hid :][None]
    results = jnp.stack(
        [
            partial_out.reshape(parts, groups, CAP, feat),
            partial_grad.reshape(parts, groups, CAP, feat),
        ],
        axis=2,
    )
    returned = lax.all_to_all(
        results[0].astype(jnp.bfloat16), "expert", split_axis=0, concat_axis=0, tiled=True
    ).astype(jnp.float32)
    combined = jnp.sum(
        returned.reshape(window, SPLIT, 2, CAP, width), axis=1, keepdims=True
    ).astype(jnp.bfloat16)
    weighted = select * slot_gate[None, :, :]
    layer_out = jnp.einsum(
        "tec,ehcf->thf", weighted, combined[:, :, 0].astype(jnp.float32), precision=HIGH
    )
    token_grad = jnp.einsum(
        "tec,ehcf->thf", select, combined[:, :, 1].astype(jnp.float32), precision=HIGH
    )
    return (
        layer_out.reshape(tok_rows, width).astype(jnp.bfloat16),
        token_grad.reshape(tok_rows, width).astype(jnp.bfloat16),
        grad_gate,
        grad_up,
        grad_down,
    )


def solution(mesh):
    return jax.shard_map(
        per_device,
        mesh=mesh,
        in_specs=(
            P(("dp", "expert"), None),
            P(("dp", "expert"), None),
            P(("dp", "expert"), None),
            P(("dp", "expert"), None),
            P("expert", "dp", None),
            P("expert", "dp", None),
            P("expert", "dp", None),
        ),
        out_specs=(
            P(("dp", "expert"), None),
            P(("dp", "expert"), None),
            P("expert", "dp", None),
            P("expert", "dp", None),
            P("expert", "dp", None),
        ),
        check_vma=False,
    )
```

profile of v0, /device:TPU:1, one launch (start us, length us, event | category | flops | bytes accessed | tf_op | source)
XLA Modules:
  0.0 262.6 jit_solution(5232182075128742454)
XLA Ops:
  7.2 0.0 copy-start
  7.2 0.8 fusion.25
  8.0 0.1 copy.38
  8.1 0.2 reduce_window_sum.11
  8.3 0.1 copy.39
  8.3 0.7 select_reduce_fusion
  9.1 0.1 select_convert_fusion
  9.2 0.1 copy.42
  9.3 0.0 copy-done
  9.3 0.2 fusion.10
  9.5 1.4 fusion.11
  10.9 0.2 maximum_bitcast_fusion.2
  11.1 0.1 copy.43
  11.2 2.9 %broadcast_in_dim.54 = bf16[4,16,2,4,3584]{4,3,2,1,0:T(4,128)(2,1)} broadcast(bf16[4,2,4,3584]{3,2,1,0:T(4,128)(2,1)S(1)} %copy.43), dimensions={0,2,3,4} | broadcast | bytes 3899392 | tf_op jit(solution)/shard_map/broadcast_in_dim | solution.py:71
  14.1 0.0 copy-start.6
  14.1 0.0 copy-start.7
  14.1 15.1 %all-to-all-start = ((bf16[64,2,4,3584]{3,2,1,0:T(4,128)(2,1)}), bf16[64,2,4,3584]{3,2,1,0:T(4,128)(2,1)}, u32[]{:S(2)}, u32[]{:S(2)}) async-start(bf16[64,2,4,3584]{3,2,1,0:T(4,128)(2,1)} %bitcast.111), calls=%async_computation | async-start | bytes 7340032 | tf_op jit(solution)/shard_map/all_to_all | solution.py:74
  29.3 0.0 copy-done.6
  29.3 0.0 copy-start.8
  29.3 26.0 %all_gather.9 = bf16[1,3584,128]{2,1,0:T(8,128)(2,1)} all-gather(bf16[1,448,128]{2,1,0:T(8,128)(2,1)S(1)} %copy-done.6), channel_id=1, replica_groups=mesh['dp'=8,'expert'=64] {'dp'}, dimensions={1}, use_global_device_ids=true | all-gather | bytes 1032192 | tf_op jit(solution)/shard_map/all_gather | solution.py:67
  55.3 0.0 copy-done.7
  55.3 24.1 %all_gather.11 = bf16[1,3584,128]{2,1,0:T(8,128)(2,1)} all-gather(bf16[1,448,128]{2,1,0:T(8,128)(2,1)S(1)} %copy-done.7), channel_id=1, replica_groups=mesh['dp'=8,'expert'=64] {'dp'}, dimensions={1}, use_global_device_ids=true | all-gather | bytes 1032192 | tf_op jit(solution)/shard_map/all_gather | solution.py:69
  79.5 0.0 copy-done.8
  79.5 24.1 %all_gather.10 = bf16[1,3584,128]{2,1,0:T(8,128)(2,1)} all-gather(bf16[1,448,128]{2,1,0:T(8,128)(2,1)S(1)} %copy-done.8), channel_id=1, replica_groups=mesh['dp'=8,'expert'=64] {'dp'}, dimensions={1}, use_global_device_ids=true | all-gather | bytes 1032192 | tf_op jit(solution)/shard_map/all_gather | solution.py:68
  103.6 10.4 %all-to-all-done = bf16[64,2,4,3584]{3,2,1,0:T(4,128)(2,1)} async-done(((bf16[64,2,4,3584]{3,2,1,0:T(4,128)(2,1)}), bf16[64,2,4,3584]{3,2,1,0:T(4,128)(2,1)}, u32[]{:S(2)}, u32[]{:S(2)}) %all-to-all-start) | async-done | bytes 3670048 | tf_op jit(solution)/shard_map/all_to_all | solution.py:74
  113.9 5.1 %fusion.42 = (bf16[1,64,1,4,3584]{4,3,2,1,0:T(4,128)(2,1)}, bf16[1,64,1,4,3584]{4,3,2,1,0:T(4,128)(2,1)}) fusion(bf16[1,64,2,4,3584]{4,3,2,1,0:T(4,128)(2,1)} %bitcast.12), kind=kLoop, calls=%fused_computation.71 | loop fusion | bytes 7340032 | tf_op jit(solution)/shard_map/slice | solution.py:77
  119.1 2.9 %reshape.115 = bf16[256,3584]{1,0:T(8,128)(2,1)S(1)} reshape(bf16[1,64,1,4,3584]{4,3,2,1,0:T(4,128)(2,1)} %get-tuple-element.21) | data formatting | bytes 3670016 | tf_op jit(solution)/shard_map/reshape.5
  122.0 4.0 %reshape.119 = bf16[256,3584]{1,0:T(8,128)(2,1)} reshape(bf16[1,64,1,4,3584]{4,3,2,1,0:T(4,128)(2,1)} %get-tuple-element.20) | data formatting | bytes 3670016 | tf_op jit(solution)/shard_map/reshape.24
  126.0 0.0 copy-start.1
  126.0 2.0 fusion.20
  128.0 0.0 copy-done.1
  128.0 0.0 copy-done.3
  128.0 0.6 fusion.12
  128.6 0.5 copy-done.5
  129.2 0.6 multiply_convert_fusion.2
  129.8 0.5 copy-done.4
  130.4 0.6 fusion.18
  131.0 1.9 fusion.2
  132.9 4.1 %stack_reshape.9 = bf16[1,64,1,4,3584]{4,3,1,2,0:T(4,128)(2,1)} reshape(bf16[1,256,3584]{2,1,0:T(8,128)(2,1)} %fusion.2) | data formatting | bytes 3670016 | tf_op jit(solution)/shard_map/stack;reshape | solution.py:85
  137.0 3.1 %fusion.1 = bf16[1,256,3584]{2,1,0:T(8,128)(2,1)} fusion(bf16[256,128]{1,0:T(8,128)(2,1)S(1)} %get-tuple-element.25, bf16[1,3584,128]{2,1,0:T(8,128)(2,1)} %all_gather.11), kind=kOutput, calls=%fused_computation.3 | convolution fusion | flops 235798528 | bytes 2818048 | tf_op jit(solution)/shard_map/rh,pfh->prf/dot_general | solution.py:31
  140.1 4.1 %stack_reshape.8 = bf16[1,64,1,4,3584]{4,3,1,2,0:T(4,128)(2,1)} reshape(bf16[1,256,3584]{2,1,0:T(8,128)(2,1)} %fusion.1) | data formatting | bytes 3670016 | tf_op jit(solution)/shard_map/stack;reshape | solution.py:85
  144.1 6.3 %maximum_bitcast_fusion = bf16[64,2,4,3584]{3,2,1,0:T(4,128)(2,1)} fusion(bf16[1,64,1,4,3584]{4,3,2,1,0:T(4,128)(2,1)} %bitcast.112, bf16[1,64,1,4,3584]{4,3,2,1,0:T(4,128)(2,1)} %bitcast.113), kind=kLoop, calls=%fused_computation.21 | loop fusion | flops 1835008 | bytes 7340032 | tf_op jit(solution)/shard_map/convert_element_type | solution.py:93
  150.4 13.0 %all-to-all-start.1 = ((bf16[64,2,4,3584]{3,2,1,0:T(4,128)(2,1)}), bf16[64,2,4,3584]{3,2,1,0:T(4,128)(2,1)}, u32[]{:S(2)}, u32[]{:S(2)}) async-start(bf16[64,2,4,3584]{3,2,1,0:T(4,128)(2,1)} %maximum_bitcast_fusion), calls=%async_computation.1 | async-start | bytes 7340032 | tf_op jit(solution)/shard_map/all_to_all | solution.py:92
  163.4 0.3 reduce-scatter.4.cloned.1.call-start
  163.7 0.5 fusion.5
  164.2 0.0 copy-start.2
  164.2 0.5 fusion.6
  164.6 1.0 copy-done.2
  165.7 0.5 fusion.7
  166.1 1.7 maximum_bitcast_fusion.1
  167.8 4.5 %copy.51 = bf16[3584,384]{1,0:T(8,128)(2,1)} copy(bf16[3584,384]{0,1:T(8,128)(2,1)} %maximum_bitcast_fusion.1) | data formatting | bytes 5505024
  172.3 0.0 reduce-scatter.4.cloned.1.call-update
  172.3 42.9 %reduce-scatter.4.cloned.1.call-done = bf16[448,384]{1,0:T(8,128)(2,1)} async-done(((bf16[3584,384]{1,0:T(8,128)(2,1)}), bf16[448,384]{1,0:T(8,128)(2,1)}) %reduce-scatter.4.cloned.1.call-update) | async-done | bytes 344080
  215.3 1.1 copy.52
  216.4 0.1 convert_element_type.96
  216.5 0.1 slice_bitcast_fusion
  216.6 0.8 copy.48
  217.4 0.8 copy.49
  218.2 0.8 copy.50
  219.0 29.1 %all-to-all-done.1 = bf16[64,2,4,3584]{3,2,1,0:T(4,128)(2,1)} async-done(((bf16[64,2,4,3584]{3,2,1,0:T(4,128)(2,1)}), bf16[64,2,4,3584]{3,2,1,0:T(4,128)(2,1)}, u32[]{:S(2)}, u32[]{:S(2)}) %all-to-all-start.1) | async-done | bytes 3670048 | tf_op jit(solution)/shard_map/all_to_all | solution.py:92
  248.1 3.6 %bitcast_reduce_fusion = bf16[4,2,4,3584]{3,2,1,0:T(4,128)(2,1)S(1)} fusion(bf16[64,2,4,3584]{3,2,1,0:T(4,128)(2,1)} %all-to-all-done.1), kind=kLoop, calls=%fused_computation.22 | loop fusion | flops 1720320 | bytes 3899392 | tf_op jit(solution)/shard_map/reduce_sum | solution.py:95
  251.7 0.1 copy.60
  251.9 1.9 fusion.4
  253.8 1.9 fusion.3
  (6 shorter events, 0.0 us)
Async XLA Ops:
  7.2 2.1 copy-start
  14.1 15.1 %copy-start.6 = (bf16[1,448,128]{2,1,0:T(8,128)(2,1)S(1)}, bf16[1,448,128]{2,1,0:T(8,128)(2,1)}, u32[]{:S(2)}) copy-start(bf16[1,448,128]{2,1,0:T(8,128)(2,1)} %param.11) | copy-start | bytes 344068
  14.1 41.2 %copy-start.7 = (bf16[1,448,128]{2,1,0:T(8,128)(2,1)S(1)}, bf16[1,448,128]{2,1,0:T(8,128)(2,1)}, u32[]{:S(2)}) copy-start(bf16[1,448,128]{2,1,0:T(8,128)(2,1)} %param.13) | copy-start | bytes 344068
  14.1 99.8 %all-to-all-start = ((bf16[64,2,4,3584]{3,2,1,0:T(4,128)(2,1)}), bf16[64,2,4,3584]{3,2,1,0:T(4,128)(2,1)}, u32[]{:S(2)}, u32[]{:S(2)}) async-start(bf16[64,2,4,3584]{3,2,1,0:T(4,128)(2,1)} %bitcast.111), calls=%async_computation | async-start | bytes 7340032 | tf_op jit(solution)/shard_map/all_to_all | solution.py:74
  29.3 50.2 %copy-start.8 = (bf16[1,448,128]{2,1,0:T(8,128)(2,1)S(1)}, bf16[1,448,128]{2,1,0:T(8,128)(2,1)}, u32[]{:S(2)}) copy-start(bf16[1,448,128]{2,1,0:T(8,128)(2,1)} %param.12) | copy-start | bytes 344068
  126.0 2.0 copy-start.1
  126.0 2.0 copy-start.3
  128.0 1.2 copy-start.5
  129.2 1.2 copy-start.4
  150.4 97.7 %all-to-all-start.1 = ((bf16[64,2,4,3584]{3,2,1,0:T(4,128)(2,1)}), bf16[64,2,4,3584]{3,2,1,0:T(4,128)(2,1)}, u32[]{:S(2)}, u32[]{:S(2)}) async-start(bf16[64,2,4,3584]{3,2,1,0:T(4,128)(2,1)} %maximum_bitcast_fusion), calls=%async_computation.1 | async-start | bytes 7340032 | tf_op jit(solution)/shard_map/all_to_all | solution.py:92
  163.4 51.8 %reduce-scatter.4.cloned.1.call-start = ((), (), s32[]{:S(2)}) async-start(), calls=%async_computation.3 | async-start | bytes 3096576
  164.2 1.5 copy-start.2
Sparse Core Ops, SparseCore 0:
  172.5 42.7 reduce-scatter.3
where the time goes:
time: 264 us; the launch traced here: 263 us
  waiting for transfers between devices  82.4 us (31%)
  blocking collectives  74.3 us (28%)
  local copies, waits for them, and re-layouts  34 us (13%)
  starting transfers between devices  28.4 us (11%)
  matrix products  15.7 us (6%)
  between operations  14.2 us (5%)
  other arithmetic  13.7 us (5%)
    unnamed x2, waiting for transfers between devices  42.9 us
    all_to_all x1, waiting for transfers between devices, per_device(): lax.all_to_all(results[0].astype(jnp.bfloat16), 'expert', split_axis=0, c...  29.1 us
    all_gather x1, blocking collectives, per_device(): lax.all_gather(w_gate, 'dp', axis=1, tiled=True)  26 us
    all_gather x1, blocking collectives, per_device(): lax.all_gather(w_down, 'dp', axis=1, tiled=True)  24.1 us
    all_gather x1, blocking collectives, per_device(): lax.all_gather(w_up, 'dp', axis=1, tiled=True)  24.1 us
    all_to_all x1, starting transfers between devices, per_device(): lax.all_to_all(outgoing, 'expert', split_axis=0, concat_axis=0, tiled=True)  15.1 us
    all_to_all x1, starting transfers between devices, per_device(): lax.all_to_all(results[0].astype(jnp.bfloat16), 'expert', split_axis=0, c...  13 us
    all_to_all x1, waiting for transfers between devices, per_device(): lax.all_to_all(outgoing, 'expert', split_axis=0, concat_axis=0, tiled=True)  10.4 us
  transfers between devices with their start and end apart: 3, of which 3 were waited for; matrix products, arithmetic and copies ran while one was open for 4% of the time, Pallas kernels for 0%

commit v1 on v0

--- a/solution.py
+++ b/solution.py
@@ -65,7 +65,9 @@
     payload = jnp.stack([slot_tokens, slot_cot], axis=2)
     gate_full, up_full, down_full = (
         lax.all_gather(w_gate, "dp", axis=1, tiled=True),
-        lax.all_gather(w_up, "dp", axis=1, tiled=True),
+        jnp.concatenate(
+            lax.all_to_all(jnp.stack([w_up] * lax.axis_size("dp")), "dp", 0, 0), axis=1
+        ),
         lax.all_gather(w_down, "dp", axis=1, tiled=True),
     )
     outgoing = jnp.broadcast_to(payload, (window, SPLIT, 2, CAP, width)).reshape(

time: 264 us -> 278 us (1.053)
  waiting for transfers between devices: 82.4 us -> 118 us
  blocking collectives: 74.3 us -> 50.2 us
    all_to_all x1, waiting for transfers between devices: 10.4 us -> 34.5 us  [per_device(): lax.all_to_all(outgoing, 'expert', split_axis=0, concat_axis=0, tiled=True)]
    all_gather x1 -> x0, blocking collectives: 24.1 us -> none  [per_device(): lax.all_gather(w_up, 'dp', axis=1, tiled=True)]
    all_to_all x0 -> x1, waiting for transfers between devices: none -> 11.8 us  [per_device(): lax.all_to_all(jnp.stack([w_up] * lax.axis_size('dp')), 'dp', 0, 0)]
    all_to_all x0 -> x1, starting transfers between devices: none -> 6.82 us  [per_device(): lax.all_to_all(jnp.stack([w_up] * lax.axis_size('dp')), 'dp', 0, 0)]
    all_to_all x1, starting transfers between devices: 13 us -> 6.26 us  [per_device(): lax.all_to_all(results[0].astype(jnp.bfloat16), 'expert', split_axis=0, c...]
    all_to_all x1, waiting for transfers between devices: 29.1 us -> 32.6 us  [per_device(): lax.all_to_all(results[0].astype(jnp.bfloat16), 'expert', split_axis=0, c...]
    unnamed x2, waiting for transfers between devices: 42.9 us -> 39.4 us
    unnamed x23 -> x21, local copies, waits for them, and re-layouts: 10.3 us -> 9.2 us
  transfers between devices with their start and end apart: 3 -> 4, of which waited for: 3 -> 4; matrix products, arithmetic and copies ran while one was open for 4% -> 9% of each run, Pallas kernels for 0% -> 0%
where the time goes in v1:
time: 278 us; the launch traced here: 277 us
  waiting for transfers between devices  118 us (42%)
  blocking collectives  50.2 us (18%)
  local copies, waits for them, and re-layouts  33.9 us (12%)
  starting transfers between devices  28.5 us (10%)
  matrix products  18.1 us (7%)
  between operations  14.2 us (5%)
  other arithmetic  13.7 us (5%)
    unnamed x2, waiting for transfers between devices  39.4 us
    all_to_all x1, waiting for transfers between devices, per_device(): lax.all_to_all(outgoing, 'expert', split_axis=0, concat_axis=0, tiled=True)  34.5 us
    all_to_all x1, waiting for transfers between devices, per_device(): lax.all_to_all(results[0].astype(jnp.bfloat16), 'expert', split_axis=0, c...  32.6 us
    all_gather x1, blocking collectives, per_device(): lax.all_gather(w_gate, 'dp', axis=1, tiled=True)  26 us
    all_gather x1, blocking collectives, per_device(): lax.all_gather(w_down, 'dp', axis=1, tiled=True)  24.1 us
    all_to_all x1, starting transfers between devices, per_device(): lax.all_to_all(outgoing, 'expert', split_axis=0, concat_axis=0, tiled=True)  15.1 us
    all_to_all x1, waiting for transfers between devices, per_device(): lax.all_to_all(jnp.stack([w_up] * lax.axis_size('dp')), 'dp', 0, 0)  11.8 us
    unnamed x21, local copies, waits for them, and re-layouts  9.2 us
  transfers between devices with their start and end apart: 4, of which 4 were waited for; matrix products, arithmetic and copies ran while one was open for 9% of the time, Pallas kernels for 0%

profile of v1, /device:TPU:1, one launch (start us, length us, event | category | flops | bytes accessed | tf_op | source)
XLA Modules:
  0.0 276.8 jit_solution(656379216648197908)
XLA Ops:
  7.2 0.0 copy-start
  7.2 0.8 fusion.22
  8.0 0.1 copy.38
  8.1 0.2 reduce_window_sum.11
  8.3 0.1 copy.39
  8.3 0.7 select_reduce_fusion
  9.1 0.1 select_convert_fusion
  9.2 0.1 copy.42
  9.3 0.0 copy-done
  9.3 0.2 fusion.10
  9.5 1.4 fusion.11
  10.9 0.2 maximum_bitcast_fusion.2
  11.1 0.1 copy.43
  11.2 2.9 %broadcast_in_dim.54 = bf16[4,16,2,4,3584]{4,3,2,1,0:T(4,128)(2,1)} broadcast(bf16[4,2,4,3584]{3,2,1,0:T(4,128)(2,1)S(1)} %copy.43), dimensions={0,2,3,4} | broadcast | bytes 3899392 | tf_op jit(solution)/shard_map/broadcast_in_dim | solution.py:73
  14.1 0.0 copy-start.5
  14.1 0.0 copy-start.6
  14.1 15.1 %all-to-all-start = ((bf16[64,2,4,3584]{3,2,1,0:T(4,128)(2,1)}), bf16[64,2,4,3584]{3,2,1,0:T(4,128)(2,1)}, u32[]{:S(2)}, u32[]{:S(2)}) async-start(bf16[64,2,4,3584]{3,2,1,0:T(4,128)(2,1)} %bitcast.108), calls=%async_computation | async-start | bytes 7340032 | tf_op jit(solution)/shard_map/all_to_all | solution.py:76
  29.3 0.0 copy-done.5
  29.3 0.0 copy-start.7
  29.3 26.0 %all_gather.6 = bf16[1,3584,128]{2,1,0:T(8,128)(2,1)} all-gather(bf16[1,448,128]{2,1,0:T(8,128)(2,1)S(1)} %copy-done.5), channel_id=1, replica_groups=mesh['dp'=8,'expert'=64] {'dp'}, dimensions={1}, use_global_device_ids=true | all-gather | bytes 1032192 | tf_op jit(solution)/shard_map/all_gather | solution.py:67
  55.3 0.0 copy-done.6
  55.3 24.1 %all_gather.7 = bf16[1,3584,128]{2,1,0:T(8,128)(2,1)} all-gather(bf16[1,448,128]{2,1,0:T(8,128)(2,1)S(1)} %copy-done.6), channel_id=1, replica_groups=mesh['dp'=8,'expert'=64] {'dp'}, dimensions={1}, use_global_device_ids=true | all-gather | bytes 1032192 | tf_op jit(solution)/shard_map/all_gather | solution.py:71
  79.4 34.5 %all-to-all-done = bf16[64,2,4,3584]{3,2,1,0:T(4,128)(2,1)} async-done(((bf16[64,2,4,3584]{3,2,1,0:T(4,128)(2,1)}), bf16[64,2,4,3584]{3,2,1,0:T(4,128)(2,1)}, u32[]{:S(2)}, u32[]{:S(2)}) %all-to-all-start) | async-done | bytes 3670048 | tf_op jit(solution)/shard_map/all_to_all | solution.py:76
  113.9 0.0 copy-done.7
  113.9 1.0 stack.27
  115.0 6.8 %all-to-all-start.1 = ((bf16[8,1,448,128]{3,2,1,0:T(8,128)(2,1)}), bf16[8,1,448,128]{3,2,1,0:T(8,128)(2,1)}, u32[]{:S(2)}, u32[]{:S(2)}) async-start(bf16[8,1,448,128]{3,2,1,0:T(8,128)(2,1)} %stack.27), calls=%async_computation.1 | async-start | bytes 1835008 | tf_op jit(solution)/shard_map/all_to_all | solution.py:69
  121.8 5.1 %fusion.39 = (bf16[1,64,1,4,3584]{4,3,2,1,0:T(4,128)(2,1)}, bf16[1,64,1,4,3584]{4,3,2,1,0:T(4,128)(2,1)}) fusion(bf16[1,64,2,4,3584]{4,3,2,1,0:T(4,128)(2,1)} %bitcast.12), kind=kLoop, calls=%fused_computation.68 | loop fusion | bytes 7340032 | tf_op jit(solution)/shard_map/slice | solution.py:79
  126.9 2.9 %reshape.121 = bf16[256,3584]{1,0:T(8,128)(2,1)S(1)} reshape(bf16[1,64,1,4,3584]{4,3,2,1,0:T(4,128)(2,1)} %get-tuple-element.21) | data formatting | bytes 3670016 | tf_op jit(solution)/shard_map/reshape.5
  129.9 4.0 %reshape.125 = bf16[256,3584]{1,0:T(8,128)(2,1)} reshape(bf16[1,64,1,4,3584]{4,3,2,1,0:T(4,128)(2,1)} %get-tuple-element.20) | data formatting | bytes 3670016 | tf_op jit(solution)/shard_map/reshape.26
  133.9 1.9 fusion.17
  135.8 0.0 copy-done.1
  135.8 0.0 copy-done.3
  135.9 0.6 fusion.12
  136.5 11.8 %all-to-all-done.1 = bf16[8,1,448,128]{3,2,1,0:T(8,128)(2,1)} async-done(((bf16[8,1,448,128]{3,2,1,0:T(8,128)(2,1)}), bf16[8,1,448,128]{3,2,1,0:T(8,128)(2,1)}, u32[]{:S(2)}, u32[]{:S(2)}) %all-to-all-start.1) | async-done | bytes 917536 | tf_op jit(solution)/shard_map/all_to_all | solution.py:69
  148.3 1.9 multiply_convert_fusion.2
  150.2 0.0 copy-done.4
  150.2 0.6 fusion.15
  150.8 3.1 %fusion.2 = bf16[1,256,3584]{2,1,0:T(8,128)(2,1)} fusion(f32[256,3584]{1,0:T(8,128)S(1)} %fusion.15, bf16[256,128]{1,0:T(8,128)(2,1)S(1)} %get-tuple-element.27, bf16[3584,128]{1,0:T(8,128)(2,1)} %bitcast.15), kind=kOutput, calls=%fused_computation.4 | convolution fusion | flops 236716032 | bytes 6488064 | tf_op jit(solution)/shard_map/rh,pfh->prf/dot_general | solution.py:37
  153.9 4.1 %stack_reshape.9 = bf16[1,64,1,4,3584]{4,3,1,2,0:T(4,128)(2,1)} reshape(bf16[1,256,3584]{2,1,0:T(8,128)(2,1)} %fusion.2) | data formatting | bytes 3670016 | tf_op jit(solution)/shard_map/stack;reshape | solution.py:87
  158.0 3.1 %fusion.1 = bf16[1,256,3584]{2,1,0:T(8,128)(2,1)} fusion(bf16[256,128]{1,0:T(8,128)(2,1)S(1)} %get-tuple-element.25, bf16[1,3584,128]{2,1,0:T(8,128)(2,1)} %all_gather.7), kind=kOutput, calls=%fused_computation.3 | convolution fusion | flops 235798528 | bytes 2818048 | tf_op jit(solution)/shard_map/rh,pfh->prf/dot_general | solution.py:31
  161.1 4.1 %stack_reshape.8 = bf16[1,64,1,4,3584]{4,3,1,2,0:T(4,128)(2,1)} reshape(bf16[1,256,3584]{2,1,0:T(8,128)(2,1)} %fusion.1) | data formatting | bytes 3670016 | tf_op jit(solution)/shard_map/stack;reshape | solution.py:87
  165.2 6.3 %maximum_bitcast_fusion = bf16[64,2,4,3584]{3,2,1,0:T(4,128)(2,1)} fusion(bf16[1,64,1,4,3584]{4,3,2,1,0:T(4,128)(2,1)} %bitcast.109, bf16[1,64,1,4,3584]{4,3,2,1,0:T(4,128)(2,1)} %bitcast.110), kind=kLoop, calls=%fused_computation.21 | loop fusion | flops 1835008 | bytes 7340032 | tf_op jit(solution)/shard_map/convert_element_type | solution.py:95
  171.4 6.3 %all-to-all-start.2 = ((bf16[64,2,4,3584]{3,2,1,0:T(4,128)(2,1)}), bf16[64,2,4,3584]{3,2,1,0:T(4,128)(2,1)}, u32[]{:S(2)}, u32[]{:S(2)}) async-start(bf16[64,2,4,3584]{3,2,1,0:T(4,128)(2,1)} %maximum_bitcast_fusion), calls=%async_computation.2 | async-start | bytes 7340032 | tf_op jit(solution)/shard_map/all_to_all | solution.py:94
  177.7 0.3 reduce-scatter.4.cloned.1.call-start
  178.0 0.5 fusion.5
  178.4 0.0 copy-start.2
  178.4 0.5 fusion.6
  178.9 1.0 copy-done.2
  179.9 0.4 fusion.7
  180.4 1.7 maximum_bitcast_fusion.1
  182.1 4.5 %copy.51 = bf16[3584,384]{1,0:T(8,128)(2,1)} copy(bf16[3584,384]{0,1:T(8,128)(2,1)} %maximum_bitcast_fusion.1) | data formatting | bytes 5505024
  186.6 0.0 reduce-scatter.4.cloned.1.call-update
  186.6 39.4 %reduce-scatter.4.cloned.1.call-done = bf16[448,384]{1,0:T(8,128)(2,1)} async-done(((bf16[3584,384]{1,0:T(8,128)(2,1)}), bf16[448,384]{1,0:T(8,128)(2,1)}) %reduce-scatter.4.cloned.1.call-update) | async-done | bytes 344080
  226.0 1.1 copy.52
  227.1 0.1 convert_element_type.96
  227.2 0.1 slice_bitcast_fusion
  227.3 0.8 copy.48
  228.1 0.8 copy.49
  228.9 0.8 copy.50
  229.8 32.6 %all-to-all-done.2 = bf16[64,2,4,3584]{3,2,1,0:T(4,128)(2,1)} async-done(((bf16[64,2,4,3584]{3,2,1,0:T(4,128)(2,1)}), bf16[64,2,4,3584]{3,2,1,0:T(4,128)(2,1)}, u32[]{:S(2)}, u32[]{:S(2)}) %all-to-all-start.2) | async-done | bytes 3670048 | tf_op jit(solution)/shard_map/all_to_all | solution.py:94
  262.4 3.6 %bitcast_reduce_fusion = bf16[4,2,4,3584]{3,2,1,0:T(4,128)(2,1)S(1)} fusion(bf16[64,2,4,3584]{3,2,1,0:T(4,128)(2,1)} %all-to-all-done.2), kind=kLoop, calls=%fused_computation.22 | loop fusion | flops 1720320 | bytes 3899392 | tf_op jit(solution)/shard_map/reduce_sum | solution.py:97
  266.0 0.1 copy.60
  266.2 1.9 fusion.4
  268.0 1.9 fusion.3
  (6 shorter events, 0.0 us)
Async XLA Ops:
  7.2 2.1 copy-start
  14.1 15.1 %copy-start.5 = (bf16[1,448,128]{2,1,0:T(8,128)(2,1)S(1)}, bf16[1,448,128]{2,1,0:T(8,128)(2,1)}, u32[]{:S(2)}) copy-start(bf16[1,448,128]{2,1,0:T(8,128)(2,1)} %param.11) | copy-start | bytes 344068
  14.1 41.2 %copy-start.6 = (bf16[1,448,128]{2,1,0:T(8,128)(2,1)S(1)}, bf16[1,448,128]{2,1,0:T(8,128)(2,1)}, u32[]{:S(2)}) copy-start(bf16[1,448,128]{2,1,0:T(8,128)(2,1)} %param.13) | copy-start | bytes 344068
  14.1 99.8 %all-to-all-start = ((bf16[64,2,4,3584]{3,2,1,0:T(4,128)(2,1)}), bf16[64,2,4,3584]{3,2,1,0:T(4,128)(2,1)}, u32[]{:S(2)}, u32[]{:S(2)}) async-start(bf16[64,2,4,3584]{3,2,1,0:T(4,128)(2,1)} %bitcast.108), calls=%async_computation | async-start | bytes 7340032 | tf_op jit(solution)/shard_map/all_to_all | solution.py:76
  29.3 84.7 %copy-start.7 = (bf16[1,448,128]{2,1,0:T(8,128)(2,1)S(1)}, bf16[1,448,128]{2,1,0:T(8,128)(2,1)}, u32[]{:S(2)}) copy-start(bf16[1,448,128]{2,1,0:T(8,128)(2,1)} %param.12) | copy-start | bytes 344068
  115.0 33.3 %all-to-all-start.1 = ((bf16[8,1,448,128]{3,2,1,0:T(8,128)(2,1)}), bf16[8,1,448,128]{3,2,1,0:T(8,128)(2,1)}, u32[]{:S(2)}, u32[]{:S(2)}) async-start(bf16[8,1,448,128]{3,2,1,0:T(8,128)(2,1)} %stack.27), calls=%async_computation.1 | async-start | bytes 1835008 | tf_op jit(solution)/shard_map/all_to_all | solution.py:69
  133.9 2.0 copy-start.1
  133.9 2.0 copy-start.3
  148.3 1.9 copy-start.4
  171.4 90.9 %all-to-all-start.2 = ((bf16[64,2,4,3584]{3,2,1,0:T(4,128)(2,1)}), bf16[64,2,4,3584]{3,2,1,0:T(4,128)(2,1)}, u32[]{:S(2)}, u32[]{:S(2)}) async-start(bf16[64,2,4,3584]{3,2,1,0:T(4,128)(2,1)} %maximum_bitcast_fusion), calls=%async_computation.2 | async-start | bytes 7340032 | tf_op jit(solution)/shard_map/all_to_all | solution.py:94
  177.7 48.3 %reduce-scatter.4.cloned.1.call-start = ((), (), s32[]{:S(2)}) async-start(), calls=%async_computation.4 | async-start | bytes 3096576
  178.4 1.5 copy-start.2
Sparse Core Ops, SparseCore 0:
  186.7 39.2 reduce-scatter.3
